TPU v7x, 32 devices: a whole 2x2x4 slice. The times are simulated.
32 devices in a mesh: starts: 2 (over y), gx: 8 (over z, x), gy: 2 (over core).
Axes of the slice: x: 2, y: 2, z: 4, core: 2. Of those that a mesh axis runs over, the one named last changes fastest.
Arguments:
- chi_final: float32 [2, 64, 128, 256], P(None, ('starts', 'gx'), 'gy'), parts along dimension 1, may hold values from -30 to 30
- psi_late: float32 [2, 64, 128, 256], P(None, ('starts', 'gx'), 'gy'), parts along dimension 1, may hold values from -0.7 to 0.7
- psi_early: float32 [2, 64, 128, 256], P(None, ('starts', 'gx'), 'gy'), parts along dimension 1, may hold values from -0.7 to 0.7
- trap: float32 [32, 128, 256], P('gx', 'gy'), may hold values from 0 to 1
- controls: float32 [4, 64, 256], P('starts', 'gy'), parts along dimension 0, may hold values from -0.5 to 0.5
Outputs:
- chi_start: float32 [2, 64, 128, 256], P(None, ('starts', 'gx'), 'gy'), parts along dimension 1
- grad_rows: float32 [4, 64, 256], P('starts', 'gy'), parts along dimension 0
- adjoint_power: float32 [2], P('starts'), parts along dimension 0
There are 2 independent parts, one for each index of `starts`. A program takes and returns all parts, laid end to end along the dimension named above; an argument that names none is the same for every part. Nothing has to cross between parts.
All inputs are finite; a program needn't handle non-finite values.
Results may differ from a plain program's by a relative error of at most 0.0005.
Values sent between devices are 32-bit elements; how exact they have to be, the bound alone decides.
No kernel may reach another device: no remote copies, remote signals or barrier semaphores. Data moves between devices by JAX's collectives and lax.ppermute only.
A program may use at most 64 MiB of HBM per device.

v0:
```python
import math
import jax
import jax.numpy as jnp
from jax import lax
from jax.sharding import PartitionSpec as P

COUPLING = 1.0
STEP_SIZE = 0.2


def extended(block, sides, width):
    for axis, dim in sides:
        count = lax.axis_size(axis)
        forward = [(i, i + 1) for i in range(count - 1)]
        backward = [(target, source) for source, target in forward]
        low = lax.ppermute(
            lax.slice_in_dim(block, block.shape[dim] - width, None, axis=dim), axis, forward
        )
        high = lax.ppermute(lax.slice_in_dim(block, 0, width, axis=dim), axis, backward)
        block = jnp.concatenate([low, block, high], axis=dim)
    return block


def coefficients(psi, trap, control, profile):
    real_part = psi[0]
    imag_part = psi[1]
    fine_control = jnp.repeat(control, 2, axis=0)
    potential = trap + profile[:, None, None] * fine_control[None, :, :]
    weight = potential + 2.0 * COUPLING * (real_part * real_part + imag_part * imag_part)
    mix_a = COUPLING * (real_part * real_part - imag_part * imag_part)
    mix_b = 2.0 * COUPLING * real_part * imag_part
    return (weight, mix_a, mix_b)


def apply_coef(lapl, field, coef):
    weight, mix_a, mix_b = coef
    real_part = field[0]
    imag_part = field[1]
    upper = -0.5 * lapl[0] + (weight + mix_a) * real_part + mix_b * imag_part
    lower = -0.5 * lapl[1] + mix_b * real_part + (weight - mix_a) * imag_part
    return jnp.stack([-lower, upper])


def operator(field, coef):
    padded = extended(field, (("gx", 1), ("gy", 2)), 1)
    z_padded = jnp.pad(field, ((0, 0), (0, 0), (0, 0), (1, 1)))
    total = padded[:, 2:, 1:-1, :] + padded[:, :-2, 1:-1, :]
    total = total + padded[:, 1:-1, 2:, :] + padded[:, 1:-1, :-2, :]
    total = total + z_padded[:, :, :, 2:] + z_padded[:, :, :, :-2]
    lapl = total - 6.0 * field
    return apply_coef(lapl, field, coef)


def rk_step(field, coef):
    section_one = operator(field, coef)
    section_two = operator(field + 0.5 * STEP_SIZE * section_one, coef)
    section_three = operator(field + 0.5 * STEP_SIZE * section_two, coef)
    section_four = operator(field + STEP_SIZE * section_three, coef)
    return field + STEP_SIZE / 6.0 * (
        section_one + 2.0 * section_two + 2.0 * section_three + section_four
    )


def row_terms(field, psi, profile):
    intersection = field[0] * psi[1] - field[1] * psi[0]
    summed = jnp.sum(intersection * profile[:, None, None], axis=0)
    return summed.reshape(summed.shape[0] // 2, 2, summed.shape[1]).sum(axis=1)


def on_device(chi_final, psi_late, psi_early, trap, controls):
    planes = chi_final.shape[1]
    width_y = chi_final.shape[2]
    depth = chi_final.shape[3]
    total_x = planes * lax.axis_size("gx")
    total_y = width_y * lax.axis_size("gy")
    first = lax.axis_index("gx") * planes
    x_index = (first + jnp.arange(planes, dtype=jnp.int32)).astype(jnp.float32)
    profile = 1.0 + 0.5 * jnp.cos(2.0 * math.pi * x_index / float(total_x))
    coef_late = coefficients(psi_late, trap, controls[1], profile)
    coef_early = coefficients(psi_early, trap, controls[0], profile)
    chi_late = rk_step(chi_final, coef_late)
    chi_start = rk_step(chi_late, coef_early)
    rows = jnp.stack(
        [row_terms(chi_start, psi_early, profile), row_terms(chi_late, psi_late, profile)]
    )
    local_sq = jnp.sum(chi_start * chi_start)
    squares = lax.psum(local_sq, ("gx", "gy"))
    rows_sum = lax.psum(rows, "gx")
    power = squares / float(total_x * total_y * depth)
    grad_rows = rows_sum / jnp.sqrt(float(total_x) * (power + 1e-06))
    return (chi_start, grad_rows, jnp.reshape(power, (1,)))


def solution(mesh):
    placed = (
        P(None, ("starts", "gx"), "gy", None),
        P(None, ("starts", "gx"), "gy", None),
        P(None, ("starts", "gx"), "gy", None),
        P("gx", "gy", None),
        P("starts", "gy", None),
    )
    return jax.shard_map(
        on_device,
        mesh=mesh,
        in_specs=placed,
        out_specs=(P(None, ("starts", "gx"), "gy", None), P("starts", "gy", None), P("starts")),
        check_vma=False,
    )
```

profile of v0, /device:TPU:0, one launch (start us, length us, event | category | flops | bytes accessed | tf_op | source)
XLA Modules:
  0.0 232.7 jit_solution(15009674649921705698)
XLA Ops:
  7.2 1.0 fusion.145
  8.3 1.3 collective-permute-start
  9.6 5.5 %collective-permute-start.1 = (f32[2,1,64,256]{3,2,1,0:T(8,128)S(1)}, f32[2,1,64,256]{3,2,1,0:T(8,128)S(1)}, u32[]{:S(2)}, u32[]{:S(2)}) collective-permute-start(f32[2,1,64,256]{3,2,1,0:T(8,128)S(1)} %get-tuple-element.62), channel_id=1, source_target_pairs={{0,2},{2,4},{4,6},{6,8},{8,10},{10,12},{12,14},{1,3},{3,5},{5,7},{... | collective-permute-start | bytes 393224 | tf_op jit(solution)/shard_map/ppermute | solution.py:16
  15.1 1.4 slice_bitcast_fusion.14
  16.5 3.1 %collective-permute-done.1 = f32[2,1,64,256]{3,2,1,0:T(8,128)S(1)} collective-permute-done((f32[2,1,64,256]{3,2,1,0:T(8,128)S(1)}, f32[2,1,64,256]{3,2,1,0:T(8,128)S(1)}, u32[]{:S(2)}, u32[]{:S(2)}) %collective-permute-start.1) | collective-permute-done | bytes 131104 | tf_op jit(solution)/shard_map/ppermute | solution.py:16
  19.7 1.3 collective-permute-start.2
  21.0 3.0 %collective-permute-start.3 = (f32[2,6,1,256]{3,2,1,0:T(1,128)S(1)}, f32[2,6,1,256]{3,2,1,0:T(1,128)S(1)}, u32[]{:S(2)}, u32[]{:S(2)}) collective-permute-start(f32[2,6,1,256]{3,2,1,0:T(1,128)S(1)} %get-tuple-element.46), channel_id=1, source_target_pairs={{0,1},{2,3},{4,5},{6,7},{8,9},{10,11},{12,13},{14,15},{16,17},{18,... | collective-permute-start | bytes 36872 | tf_op jit(solution)/shard_map/ppermute | solution.py:16
  24.2 0.6 collective-permute-done.3
  25.7 4.4 %collective-permute-start.5 = (f32[2,1,64,256]{3,2,1,0:T(8,128)S(1)}, f32[2,1,64,256]{3,2,1,0:T(8,128)S(1)}, u32[]{:S(2)}, u32[]{:S(2)}) collective-permute-start(f32[2,1,64,256]{3,2,1,0:T(8,128)S(1)} %get-tuple-element.59), channel_id=1, source_target_pairs={{0,2},{2,4},{4,6},{6,8},{8,10},{10,12},{12,14},{1,3},{3,5},{5,7},{... | collective-permute-start | bytes 393224 | tf_op jit(solution)/shard_map/ppermute | solution.py:16
  30.1 1.3 collective-permute-start.4
  31.4 1.9 collective-permute-done.5
  33.3 4.1 %collective-permute-done.4 = f32[2,1,64,256]{3,2,1,0:T(8,128)S(1)} collective-permute-done((f32[2,1,64,256]{3,2,1,0:T(8,128)S(1)}, f32[2,1,64,256]{3,2,1,0:T(8,128)S(1)}, u32[]{:S(2)}, u32[]{:S(2)}) %collective-permute-start.4) | collective-permute-done | bytes 131104 | tf_op jit(solution)/shard_map/ppermute | solution.py:19
  37.5 1.3 collective-permute-start.6
  38.8 3.0 %collective-permute-start.7 = (f32[2,6,1,256]{3,2,1,0:T(1,128)S(1)}, f32[2,6,1,256]{3,2,1,0:T(1,128)S(1)}, u32[]{:S(2)}, u32[]{:S(2)}) collective-permute-start(f32[2,6,1,256]{3,2,1,0:T(1,128)S(1)} %get-tuple-element.44), channel_id=1, source_target_pairs={{0,1},{2,3},{4,5},{6,7},{8,9},{10,11},{12,13},{14,15},{16,17},{18,... | collective-permute-start | bytes 36872 | tf_op jit(solution)/shard_map/ppermute | solution.py:16
  41.9 0.8 collective-permute-done.7
  43.3 4.5 %collective-permute-start.9 = (f32[2,1,64,256]{3,2,1,0:T(8,128)S(1)}, f32[2,1,64,256]{3,2,1,0:T(8,128)S(1)}, u32[]{:S(2)}, u32[]{:S(2)}) collective-permute-start(f32[2,1,64,256]{3,2,1,0:T(8,128)S(1)} %get-tuple-element.57), channel_id=1, source_target_pairs={{0,2},{2,4},{4,6},{6,8},{8,10},{10,12},{12,14},{1,3},{3,5},{5,7},{... | collective-permute-start | bytes 393224 | tf_op jit(solution)/shard_map/ppermute | solution.py:16
  47.9 1.3 collective-permute-start.8
  49.2 1.9 collective-permute-done.9
  51.1 4.1 %collective-permute-done.8 = f32[2,1,64,256]{3,2,1,0:T(8,128)S(1)} collective-permute-done((f32[2,1,64,256]{3,2,1,0:T(8,128)S(1)}, f32[2,1,64,256]{3,2,1,0:T(8,128)S(1)}, u32[]{:S(2)}, u32[]{:S(2)}) %collective-permute-start.8) | collective-permute-done | bytes 131104 | tf_op jit(solution)/shard_map/ppermute | solution.py:19
  55.2 1.3 collective-permute-start.10
  56.5 3.0 %collective-permute-start.11 = (f32[2,6,1,256]{3,2,1,0:T(1,128)S(1)}, f32[2,6,1,256]{3,2,1,0:T(1,128)S(1)}, u32[]{:S(2)}, u32[]{:S(2)}) collective-permute-start(f32[2,6,1,256]{3,2,1,0:T(1,128)S(1)} %get-tuple-element.42), channel_id=1, source_target_pairs={{0,1},{2,3},{4,5},{6,7},{8,9},{10,11},{12,13},{14,15},{16,17},{18,... | collective-permute-start | bytes 36872 | tf_op jit(solution)/shard_map/ppermute | solution.py:16
  59.6 0.8 collective-permute-done.11
  61.0 4.0 %collective-permute-start.13 = (f32[2,1,64,256]{3,2,1,0:T(8,128)S(1)}, f32[2,1,64,256]{3,2,1,0:T(8,128)S(1)}, u32[]{:S(2)}, u32[]{:S(2)}) collective-permute-start(f32[2,1,64,256]{3,2,1,0:T(8,128)S(1)} %get-tuple-element.55), channel_id=1, source_target_pairs={{0,2},{2,4},{4,6},{6,8},{8,10},{10,12},{12,14},{1,3},{3,5},{5,7},{... | collective-permute-start | bytes 393224 | tf_op jit(solution)/shard_map/ppermute | solution.py:16
  65.0 1.3 collective-permute-start.12
  66.3 1.9 collective-permute-done.13
  68.2 4.1 %collective-permute-done.12 = f32[2,1,64,256]{3,2,1,0:T(8,128)S(1)} collective-permute-done((f32[2,1,64,256]{3,2,1,0:T(8,128)S(1)}, f32[2,1,64,256]{3,2,1,0:T(8,128)S(1)}, u32[]{:S(2)}, u32[]{:S(2)}) %collective-permute-start.12) | collective-permute-done | bytes 131104 | tf_op jit(solution)/shard_map/ppermute | solution.py:19
  72.4 1.3 collective-permute-start.14
  73.7 3.0 %collective-permute-start.15 = (f32[2,6,1,256]{3,2,1,0:T(1,128)S(1)}, f32[2,6,1,256]{3,2,1,0:T(1,128)S(1)}, u32[]{:S(2)}, u32[]{:S(2)}) collective-permute-start(f32[2,6,1,256]{3,2,1,0:T(1,128)S(1)} %get-tuple-element.40), channel_id=1, source_target_pairs={{0,1},{2,3},{4,5},{6,7},{8,9},{10,11},{12,13},{14,15},{16,17},{18,... | collective-permute-start | bytes 36872 | tf_op jit(solution)/shard_map/ppermute | solution.py:16
  76.7 0.8 collective-permute-done.15
  78.2 4.0 %collective-permute-start.17 = (f32[2,1,64,256]{3,2,1,0:T(8,128)S(1)}, f32[2,1,64,256]{3,2,1,0:T(8,128)S(1)}, u32[]{:S(2)}, u32[]{:S(2)}) collective-permute-start(f32[2,1,64,256]{3,2,1,0:T(8,128)S(1)} %get-tuple-element.53), channel_id=1, source_target_pairs={{0,2},{2,4},{4,6},{6,8},{8,10},{10,12},{12,14},{1,3},{3,5},{5,7},{... | collective-permute-start | bytes 393224 | tf_op jit(solution)/shard_map/ppermute | solution.py:16
  82.3 1.3 collective-permute-start.16
  83.6 1.9 collective-permute-done.17
  85.5 4.1 %collective-permute-done.16 = f32[2,1,64,256]{3,2,1,0:T(8,128)S(1)} collective-permute-done((f32[2,1,64,256]{3,2,1,0:T(8,128)S(1)}, f32[2,1,64,256]{3,2,1,0:T(8,128)S(1)}, u32[]{:S(2)}, u32[]{:S(2)}) %collective-permute-start.16) | collective-permute-done | bytes 131104 | tf_op jit(solution)/shard_map/ppermute | solution.py:19
  89.6 0.6 pad_maximum_fusion.78
  90.3 1.3 collective-permute-start.18
  91.6 4.2 %collective-permute-start.19 = (f32[2,6,1,256]{3,2,1,0:T(1,128)S(1)}, f32[2,6,1,256]{3,2,1,0:T(1,128)}, u32[]{:S(2)}, u32[]{:S(2)}) collective-permute-start(f32[2,6,1,256]{3,2,1,0:T(1,128)S(1)} %get-tuple-element.38), channel_id=1, source_target_pairs={{0,1},{2,3},{4,5},{6,7},{8,9},{10,11},{12,13},{14,15},{16,17},{18,... | collective-permute-start | bytes 36872 | tf_op jit(solution)/shard_map/ppermute | solution.py:16
  95.8 0.7 broadcast_in_dim.5
  96.4 1.5 mul.427
  97.9 1.3 fusion.14
  100.0 4.0 %collective-permute-start.21 = (f32[2,1,64,256]{3,2,1,0:T(8,128)S(1)}, f32[2,1,64,256]{3,2,1,0:T(8,128)S(1)}, u32[]{:S(2)}, u32[]{:S(2)}) collective-permute-start(f32[2,1,64,256]{3,2,1,0:T(8,128)S(1)} %get-tuple-element.51), channel_id=1, source_target_pairs={{0,2},{2,4},{4,6},{6,8},{8,10},{10,12},{12,14},{1,3},{3,5},{5,7},{... | collective-permute-start | bytes 393224 | tf_op jit(solution)/shard_map/ppermute | solution.py:16
  103.9 1.3 collective-permute-start.20
  105.2 1.2 collective-permute-done.21
  106.4 4.4 %collective-permute-done.20 = f32[2,1,64,256]{3,2,1,0:T(8,128)S(1)} collective-permute-done((f32[2,1,64,256]{3,2,1,0:T(8,128)S(1)}, f32[2,1,64,256]{3,2,1,0:T(8,128)S(1)}, u32[]{:S(2)}, u32[]{:S(2)}) %collective-permute-start.20) | collective-permute-done | bytes 131104 | tf_op jit(solution)/shard_map/ppermute | solution.py:19
  110.8 1.3 collective-permute-start.22
  112.1 3.0 %collective-permute-start.23 = (f32[2,6,1,256]{3,2,1,0:T(1,128)S(1)}, f32[2,6,1,256]{3,2,1,0:T(1,128)S(1)}, u32[]{:S(2)}, u32[]{:S(2)}) collective-permute-start(f32[2,6,1,256]{3,2,1,0:T(1,128)S(1)} %get-tuple-element.36), channel_id=1, source_target_pairs={{0,1},{2,3},{4,5},{6,7},{8,9},{10,11},{12,13},{14,15},{16,17},{18,... | collective-permute-start | bytes 36872 | tf_op jit(solution)/shard_map/ppermute | solution.py:16
  115.2 0.8 collective-permute-done.23
  116.8 4.0 %collective-permute-start.25 = (f32[2,1,64,256]{3,2,1,0:T(8,128)S(1)}, f32[2,1,64,256]{3,2,1,0:T(8,128)S(1)}, u32[]{:S(2)}, u32[]{:S(2)}) collective-permute-start(f32[2,1,64,256]{3,2,1,0:T(8,128)S(1)} %get-tuple-element.49), channel_id=1, source_target_pairs={{0,2},{2,4},{4,6},{6,8},{8,10},{10,12},{12,14},{1,3},{3,5},{5,7},{... | collective-permute-start | bytes 393224 | tf_op jit(solution)/shard_map/ppermute | solution.py:16
  120.8 1.3 collective-permute-start.24
  122.1 1.9 collective-permute-done.25
  124.0 4.1 %collective-permute-done.24 = f32[2,1,64,256]{3,2,1,0:T(8,128)S(1)} collective-permute-done((f32[2,1,64,256]{3,2,1,0:T(8,128)S(1)}, f32[2,1,64,256]{3,2,1,0:T(8,128)S(1)}, u32[]{:S(2)}, u32[]{:S(2)}) %collective-permute-start.24) | collective-permute-done | bytes 131104 | tf_op jit(solution)/shard_map/ppermute | solution.py:19
  128.1 1.3 collective-permute-start.26
  129.4 3.0 %collective-permute-start.27 = (f32[2,6,1,256]{3,2,1,0:T(1,128)S(1)}, f32[2,6,1,256]{3,2,1,0:T(1,128)S(1)}, u32[]{:S(2)}, u32[]{:S(2)}) collective-permute-start(f32[2,6,1,256]{3,2,1,0:T(1,128)S(1)} %get-tuple-element.34), channel_id=1, source_target_pairs={{0,1},{2,3},{4,5},{6,7},{8,9},{10,11},{12,13},{14,15},{16,17},{18,... | collective-permute-start | bytes 36872 | tf_op jit(solution)/shard_map/ppermute | solution.py:16
  132.5 0.8 collective-permute-done.27
  134.1 3.8 %collective-permute-start.29 = (f32[2,1,64,256]{3,2,1,0:T(8,128)S(1)}, f32[2,1,64,256]{3,2,1,0:T(8,128)S(1)}, u32[]{:S(2)}, u32[]{:S(2)}) collective-permute-start(f32[2,1,64,256]{3,2,1,0:T(8,128)S(1)} %get-tuple-element.47), channel_id=1, source_target_pairs={{0,2},{2,4},{4,6},{6,8},{8,10},{10,12},{12,14},{1,3},{3,5},{5,7},{... | collective-permute-start | bytes 393224 | tf_op jit(solution)/shard_map/ppermute | solution.py:16
  137.9 1.3 collective-permute-start.28
  139.2 1.9 collective-permute-done.29
  141.1 4.1 %collective-permute-done.28 = f32[2,1,64,256]{3,2,1,0:T(8,128)S(1)} collective-permute-done((f32[2,1,64,256]{3,2,1,0:T(8,128)S(1)}, f32[2,1,64,256]{3,2,1,0:T(8,128)S(1)}, u32[]{:S(2)}, u32[]{:S(2)}) %collective-permute-start.28) | collective-permute-done | bytes 131104 | tf_op jit(solution)/shard_map/ppermute | solution.py:19
  145.3 1.3 collective-permute-start.30
  146.6 3.0 %collective-permute-start.31 = (f32[2,6,1,256]{3,2,1,0:T(1,128)S(1)}, f32[2,6,1,256]{3,2,1,0:T(1,128)S(1)}, u32[]{:S(2)}, u32[]{:S(2)}) collective-permute-start(f32[2,6,1,256]{3,2,1,0:T(1,128)S(1)} %get-tuple-element.32), channel_id=1, source_target_pairs={{0,1},{2,3},{4,5},{6,7},{8,9},{10,11},{12,13},{14,15},{16,17},{18,... | collective-permute-start | bytes 36872 | tf_op jit(solution)/shard_map/ppermute | solution.py:16
  149.6 0.8 collective-permute-done.31
  150.9 1.1 multiply_reduce_fusion
  153.7 32.3 %psum.15 = f32[]{:T(128)} all-reduce(f32[]{:T(128)} %get-tuple-element.5), channel_id=1, replica_groups=mesh['starts'=2,'gx'=8,'gy'=2] {'gx','gy'}, use_global_device_ids=true, to_apply=%region_6.7 | all-reduce | flops 1 | bytes 8 | tf_op jit(solution)/shard_map/psum | solution.py:87
  186.7 36.6 %all-reduce.10.cloned.1.call-done = f32[2,32,256]{2,1,0:T(8,128)} async-done(((f32[2,32,256]{2,1,0:T(8,128)}), f32[2,32,256]{2,1,0:T(8,128)}) %all-reduce.10.cloned.1.call-update) | async-done | bytes 65552 | tf_op jit(solution)/shard_map/psum | solution.py:88
  223.3 1.5 broadcast_divide_fusion
  (80 shorter events, 7.5 us)
Async XLA Ops:
  7.2 12.4 %copy-start = (f32[2,4,64,256]{3,2,1,0:T(8,128)S(1)}, f32[2,4,64,256]{3,2,1,0:T(8,128)}, u32[]{:S(2)}) copy-start(f32[2,4,64,256]{3,2,1,0:T(8,128)} %param.5) | copy-start | bytes 1572868
  7.2 216.1 %all-reduce.10.cloned.1.call-start = ((), (), s32[]{:S(2)}) async-start(), calls=%async_computation | async-start | bytes 131072 | tf_op jit(solution)/shard_map/psum | solution.py:88
  8.3 11.4 %collective-permute-start = (f32[2,1,64,256]{3,2,1,0:T(8,128)S(1)}, f32[2,1,64,256]{3,2,1,0:T(8,128)S(1)}, u32[]{:S(2)}, u32[]{:S(2)}) collective-permute-start(f32[2,1,64,256]{3,2,1,0:T(8,128)S(1)} %get-tuple-element.61), channel_id=1, source_target_pairs={{2,0},{4,2},{6,4},{8,6},{10,8},{12,10},{14,12},{3,1},{5,3},{7,5},{... | collective-permute-start | bytes 393224 | tf_op jit(solution)/shard_map/ppermute | solution.py:19
  9.6 10.0 %collective-permute-start.1 = (f32[2,1,64,256]{3,2,1,0:T(8,128)S(1)}, f32[2,1,64,256]{3,2,1,0:T(8,128)S(1)}, u32[]{:S(2)}, u32[]{:S(2)}) collective-permute-start(f32[2,1,64,256]{3,2,1,0:T(8,128)S(1)} %get-tuple-element.62), channel_id=1, source_target_pairs={{0,2},{2,4},{4,6},{6,8},{8,10},{10,12},{12,14},{1,3},{3,5},{5,7},{... | collective-permute-start | bytes 393224 | tf_op jit(solution)/shard_map/ppermute | solution.py:16
  19.7 4.5 %collective-permute-start.2 = (f32[2,6,1,256]{3,2,1,0:T(1,128)S(1)}, f32[2,6,1,256]{3,2,1,0:T(1,128)S(1)}, u32[]{:S(2)}, u32[]{:S(2)}) collective-permute-start(f32[2,6,1,256]{3,2,1,0:T(1,128)S(1)} %get-tuple-element.45), channel_id=1, source_target_pairs={{1,0},{3,2},{5,4},{7,6},{9,8},{11,10},{13,12},{15,14},{17,16},{19,... | collective-permute-start | bytes 36872 | tf_op jit(solution)/shard_map/ppermute | solution.py:19
  21.0 3.9 %collective-permute-start.3 = (f32[2,6,1,256]{3,2,1,0:T(1,128)S(1)}, f32[2,6,1,256]{3,2,1,0:T(1,128)S(1)}, u32[]{:S(2)}, u32[]{:S(2)}) collective-permute-start(f32[2,6,1,256]{3,2,1,0:T(1,128)S(1)} %get-tuple-element.46), channel_id=1, source_target_pairs={{0,1},{2,3},{4,5},{6,7},{8,9},{10,11},{12,13},{14,15},{16,17},{18,... | collective-permute-start | bytes 36872 | tf_op jit(solution)/shard_map/ppermute | solution.py:16
  24.2 1.1 copy-start.1
  24.2 1.1 copy-start.5
  25.7 7.6 %collective-permute-start.5 = (f32[2,1,64,256]{3,2,1,0:T(8,128)S(1)}, f32[2,1,64,256]{3,2,1,0:T(8,128)S(1)}, u32[]{:S(2)}, u32[]{:S(2)}) collective-permute-start(f32[2,1,64,256]{3,2,1,0:T(8,128)S(1)} %get-tuple-element.59), channel_id=1, source_target_pairs={{0,2},{2,4},{4,6},{6,8},{8,10},{10,12},{12,14},{1,3},{3,5},{5,7},{... | collective-permute-start | bytes 393224 | tf_op jit(solution)/shard_map/ppermute | solution.py:16
  30.1 7.4 %collective-permute-start.4 = (f32[2,1,64,256]{3,2,1,0:T(8,128)S(1)}, f32[2,1,64,256]{3,2,1,0:T(8,128)S(1)}, u32[]{:S(2)}, u32[]{:S(2)}) collective-permute-start(f32[2,1,64,256]{3,2,1,0:T(8,128)S(1)} %get-tuple-element.60), channel_id=1, source_target_pairs={{2,0},{4,2},{6,4},{8,6},{10,8},{12,10},{14,12},{3,1},{5,3},{7,5},{... | collective-permute-start | bytes 393224 | tf_op jit(solution)/shard_map/ppermute | solution.py:19
  37.5 4.3 %collective-permute-start.6 = (f32[2,6,1,256]{3,2,1,0:T(1,128)S(1)}, f32[2,6,1,256]{3,2,1,0:T(1,128)S(1)}, u32[]{:S(2)}, u32[]{:S(2)}) collective-permute-start(f32[2,6,1,256]{3,2,1,0:T(1,128)S(1)} %get-tuple-element.43), channel_id=1, source_target_pairs={{1,0},{3,2},{5,4},{7,6},{9,8},{11,10},{13,12},{15,14},{17,16},{19,... | collective-permute-start | bytes 36872 | tf_op jit(solution)/shard_map/ppermute | solution.py:19
  38.8 3.9 %collective-permute-start.7 = (f32[2,6,1,256]{3,2,1,0:T(1,128)S(1)}, f32[2,6,1,256]{3,2,1,0:T(1,128)S(1)}, u32[]{:S(2)}, u32[]{:S(2)}) collective-permute-start(f32[2,6,1,256]{3,2,1,0:T(1,128)S(1)} %get-tuple-element.44), channel_id=1, source_target_pairs={{0,1},{2,3},{4,5},{6,7},{8,9},{10,11},{12,13},{14,15},{16,17},{18,... | collective-permute-start | bytes 36872 | tf_op jit(solution)/shard_map/ppermute | solution.py:16
  43.3 7.8 %collective-permute-start.9 = (f32[2,1,64,256]{3,2,1,0:T(8,128)S(1)}, f32[2,1,64,256]{3,2,1,0:T(8,128)S(1)}, u32[]{:S(2)}, u32[]{:S(2)}) collective-permute-start(f32[2,1,64,256]{3,2,1,0:T(8,128)S(1)} %get-tuple-element.57), channel_id=1, source_target_pairs={{0,2},{2,4},{4,6},{6,8},{8,10},{10,12},{12,14},{1,3},{3,5},{5,7},{... | collective-permute-start | bytes 393224 | tf_op jit(solution)/shard_map/ppermute | solution.py:16
  47.9 7.4 %collective-permute-start.8 = (f32[2,1,64,256]{3,2,1,0:T(8,128)S(1)}, f32[2,1,64,256]{3,2,1,0:T(8,128)S(1)}, u32[]{:S(2)}, u32[]{:S(2)}) collective-permute-start(f32[2,1,64,256]{3,2,1,0:T(8,128)S(1)} %get-tuple-element.58), channel_id=1, source_target_pairs={{2,0},{4,2},{6,4},{8,6},{10,8},{12,10},{14,12},{3,1},{5,3},{7,5},{... | collective-permute-start | bytes 393224 | tf_op jit(solution)/shard_map/ppermute | solution.py:19
  55.2 4.3 %collective-permute-start.10 = (f32[2,6,1,256]{3,2,1,0:T(1,128)S(1)}, f32[2,6,1,256]{3,2,1,0:T(1,128)S(1)}, u32[]{:S(2)}, u32[]{:S(2)}) collective-permute-start(f32[2,6,1,256]{3,2,1,0:T(1,128)S(1)} %get-tuple-element.41), channel_id=1, source_target_pairs={{1,0},{3,2},{5,4},{7,6},{9,8},{11,10},{13,12},{15,14},{17,16},{19,... | collective-permute-start | bytes 36872 | tf_op jit(solution)/shard_map/ppermute | solution.py:19
  56.5 3.9 %collective-permute-start.11 = (f32[2,6,1,256]{3,2,1,0:T(1,128)S(1)}, f32[2,6,1,256]{3,2,1,0:T(1,128)S(1)}, u32[]{:S(2)}, u32[]{:S(2)}) collective-permute-start(f32[2,6,1,256]{3,2,1,0:T(1,128)S(1)} %get-tuple-element.42), channel_id=1, source_target_pairs={{0,1},{2,3},{4,5},{6,7},{8,9},{10,11},{12,13},{14,15},{16,17},{18,... | collective-permute-start | bytes 36872 | tf_op jit(solution)/shard_map/ppermute | solution.py:16
  61.0 7.2 %collective-permute-start.13 = (f32[2,1,64,256]{3,2,1,0:T(8,128)S(1)}, f32[2,1,64,256]{3,2,1,0:T(8,128)S(1)}, u32[]{:S(2)}, u32[]{:S(2)}) collective-permute-start(f32[2,1,64,256]{3,2,1,0:T(8,128)S(1)} %get-tuple-element.55), channel_id=1, source_target_pairs={{0,2},{2,4},{4,6},{6,8},{8,10},{10,12},{12,14},{1,3},{3,5},{5,7},{... | collective-permute-start | bytes 393224 | tf_op jit(solution)/shard_map/ppermute | solution.py:16
  65.0 7.4 %collective-permute-start.12 = (f32[2,1,64,256]{3,2,1,0:T(8,128)S(1)}, f32[2,1,64,256]{3,2,1,0:T(8,128)S(1)}, u32[]{:S(2)}, u32[]{:S(2)}) collective-permute-start(f32[2,1,64,256]{3,2,1,0:T(8,128)S(1)} %get-tuple-element.56), channel_id=1, source_target_pairs={{2,0},{4,2},{6,4},{8,6},{10,8},{12,10},{14,12},{3,1},{5,3},{7,5},{... | collective-permute-start | bytes 393224 | tf_op jit(solution)/shard_map/ppermute | solution.py:19
  72.4 4.3 %collective-permute-start.14 = (f32[2,6,1,256]{3,2,1,0:T(1,128)S(1)}, f32[2,6,1,256]{3,2,1,0:T(1,128)S(1)}, u32[]{:S(2)}, u32[]{:S(2)}) collective-permute-start(f32[2,6,1,256]{3,2,1,0:T(1,128)S(1)} %get-tuple-element.39), channel_id=1, source_target_pairs={{1,0},{3,2},{5,4},{7,6},{9,8},{11,10},{13,12},{15,14},{17,16},{19,... | collective-permute-start | bytes 36872 | tf_op jit(solution)/shard_map/ppermute | solution.py:19
  73.7 3.9 %collective-permute-start.15 = (f32[2,6,1,256]{3,2,1,0:T(1,128)S(1)}, f32[2,6,1,256]{3,2,1,0:T(1,128)S(1)}, u32[]{:S(2)}, u32[]{:S(2)}) collective-permute-start(f32[2,6,1,256]{3,2,1,0:T(1,128)S(1)} %get-tuple-element.40), channel_id=1, source_target_pairs={{0,1},{2,3},{4,5},{6,7},{8,9},{10,11},{12,13},{14,15},{16,17},{18,... | collective-permute-start | bytes 36872 | tf_op jit(solution)/shard_map/ppermute | solution.py:16
  78.2 7.2 %collective-permute-start.17 = (f32[2,1,64,256]{3,2,1,0:T(8,128)S(1)}, f32[2,1,64,256]{3,2,1,0:T(8,128)S(1)}, u32[]{:S(2)}, u32[]{:S(2)}) collective-permute-start(f32[2,1,64,256]{3,2,1,0:T(8,128)S(1)} %get-tuple-element.53), channel_id=1, source_target_pairs={{0,2},{2,4},{4,6},{6,8},{8,10},{10,12},{12,14},{1,3},{3,5},{5,7},{... | collective-permute-start | bytes 393224 | tf_op jit(solution)/shard_map/ppermute | solution.py:16
  82.2 13.5 %copy-start.8 = (f32[32,256]{1,0:T(8,128)S(1)}, f32[32,256]{1,0:T(8,128)}, u32[]{:S(2)}) copy-start(f32[32,256]{1,0:T(8,128)} %get-tuple-element.63) | copy-start | bytes 98308
  82.3 7.4 %collective-permute-start.16 = (f32[2,1,64,256]{3,2,1,0:T(8,128)S(1)}, f32[2,1,64,256]{3,2,1,0:T(8,128)S(1)}, u32[]{:S(2)}, u32[]{:S(2)}) collective-permute-start(f32[2,1,64,256]{3,2,1,0:T(8,128)S(1)} %get-tuple-element.54), channel_id=1, source_target_pairs={{2,0},{4,2},{6,4},{8,6},{10,8},{12,10},{14,12},{3,1},{5,3},{7,5},{... | collective-permute-start | bytes 393224 | tf_op jit(solution)/shard_map/ppermute | solution.py:19
  89.6 0.7 copy-start.6
  90.3 7.7 %collective-permute-start.18 = (f32[2,6,1,256]{3,2,1,0:T(1,128)}, f32[2,6,1,256]{3,2,1,0:T(1,128)}, u32[]{:S(2)}, u32[]{:S(2)}) collective-permute-start(f32[2,6,1,256]{3,2,1,0:T(1,128)} %get-tuple-element.37), channel_id=1, source_target_pairs={{1,0},{3,2},{5,4},{7,6},{9,8},{11,10},{13,12},{15,14},{17,16},{19,... | collective-permute-start | bytes 36872 | tf_op jit(solution)/shard_map/ppermute | solution.py:19
  91.6 6.4 %collective-permute-start.19 = (f32[2,6,1,256]{3,2,1,0:T(1,128)S(1)}, f32[2,6,1,256]{3,2,1,0:T(1,128)}, u32[]{:S(2)}, u32[]{:S(2)}) collective-permute-start(f32[2,6,1,256]{3,2,1,0:T(1,128)S(1)} %get-tuple-element.38), channel_id=1, source_target_pairs={{0,1},{2,3},{4,5},{6,7},{8,9},{10,11},{12,13},{14,15},{16,17},{18,... | collective-permute-start | bytes 36872 | tf_op jit(solution)/shard_map/ppermute | solution.py:16
  97.9 1.3 copy-start.3
  97.9 1.4 copy-start.7
  100.0 6.5 %collective-permute-start.21 = (f32[2,1,64,256]{3,2,1,0:T(8,128)S(1)}, f32[2,1,64,256]{3,2,1,0:T(8,128)S(1)}, u32[]{:S(2)}, u32[]{:S(2)}) collective-permute-start(f32[2,1,64,256]{3,2,1,0:T(8,128)S(1)} %get-tuple-element.51), channel_id=1, source_target_pairs={{0,2},{2,4},{4,6},{6,8},{8,10},{10,12},{12,14},{1,3},{3,5},{5,7},{... | collective-permute-start | bytes 393224 | tf_op jit(solution)/shard_map/ppermute | solution.py:16
  103.9 6.9 %collective-permute-start.20 = (f32[2,1,64,256]{3,2,1,0:T(8,128)S(1)}, f32[2,1,64,256]{3,2,1,0:T(8,128)S(1)}, u32[]{:S(2)}, u32[]{:S(2)}) collective-permute-start(f32[2,1,64,256]{3,2,1,0:T(8,128)S(1)} %get-tuple-element.52), channel_id=1, source_target_pairs={{2,0},{4,2},{6,4},{8,6},{10,8},{12,10},{14,12},{3,1},{5,3},{7,5},{... | collective-permute-start | bytes 393224 | tf_op jit(solution)/shard_map/ppermute | solution.py:19
  110.8 4.3 %collective-permute-start.22 = (f32[2,6,1,256]{3,2,1,0:T(1,128)S(1)}, f32[2,6,1,256]{3,2,1,0:T(1,128)S(1)}, u32[]{:S(2)}, u32[]{:S(2)}) collective-permute-start(f32[2,6,1,256]{3,2,1,0:T(1,128)S(1)} %get-tuple-element.35), channel_id=1, source_target_pairs={{1,0},{3,2},{5,4},{7,6},{9,8},{11,10},{13,12},{15,14},{17,16},{19,... | collective-permute-start | bytes 36872 | tf_op jit(solution)/shard_map/ppermute | solution.py:19
  112.1 3.9 %collective-permute-start.23 = (f32[2,6,1,256]{3,2,1,0:T(1,128)S(1)}, f32[2,6,1,256]{3,2,1,0:T(1,128)S(1)}, u32[]{:S(2)}, u32[]{:S(2)}) collective-permute-start(f32[2,6,1,256]{3,2,1,0:T(1,128)S(1)} %get-tuple-element.36), channel_id=1, source_target_pairs={{0,1},{2,3},{4,5},{6,7},{8,9},{10,11},{12,13},{14,15},{16,17},{18,... | collective-permute-start | bytes 36872 | tf_op jit(solution)/shard_map/ppermute | solution.py:16
  116.8 7.2 %collective-permute-start.25 = (f32[2,1,64,256]{3,2,1,0:T(8,128)S(1)}, f32[2,1,64,256]{3,2,1,0:T(8,128)S(1)}, u32[]{:S(2)}, u32[]{:S(2)}) collective-permute-start(f32[2,1,64,256]{3,2,1,0:T(8,128)S(1)} %get-tuple-element.49), channel_id=1, source_target_pairs={{0,2},{2,4},{4,6},{6,8},{8,10},{10,12},{12,14},{1,3},{3,5},{5,7},{... | collective-permute-start | bytes 393224 | tf_op jit(solution)/shard_map/ppermute | solution.py:16
  120.8 7.4 %collective-permute-start.24 = (f32[2,1,64,256]{3,2,1,0:T(8,128)S(1)}, f32[2,1,64,256]{3,2,1,0:T(8,128)S(1)}, u32[]{:S(2)}, u32[]{:S(2)}) collective-permute-start(f32[2,1,64,256]{3,2,1,0:T(8,128)S(1)} %get-tuple-element.50), channel_id=1, source_target_pairs={{2,0},{4,2},{6,4},{8,6},{10,8},{12,10},{14,12},{3,1},{5,3},{7,5},{... | collective-permute-start | bytes 393224 | tf_op jit(solution)/shard_map/ppermute | solution.py:19
  128.1 4.3 %collective-permute-start.26 = (f32[2,6,1,256]{3,2,1,0:T(1,128)S(1)}, f32[2,6,1,256]{3,2,1,0:T(1,128)S(1)}, u32[]{:S(2)}, u32[]{:S(2)}) collective-permute-start(f32[2,6,1,256]{3,2,1,0:T(1,128)S(1)} %get-tuple-element.33), channel_id=1, source_target_pairs={{1,0},{3,2},{5,4},{7,6},{9,8},{11,10},{13,12},{15,14},{17,16},{19,... | collective-permute-start | bytes 36872 | tf_op jit(solution)/shard_map/ppermute | solution.py:19
  129.4 3.9 %collective-permute-start.27 = (f32[2,6,1,256]{3,2,1,0:T(1,128)S(1)}, f32[2,6,1,256]{3,2,1,0:T(1,128)S(1)}, u32[]{:S(2)}, u32[]{:S(2)}) collective-permute-start(f32[2,6,1,256]{3,2,1,0:T(1,128)S(1)} %get-tuple-element.34), channel_id=1, source_target_pairs={{0,1},{2,3},{4,5},{6,7},{8,9},{10,11},{12,13},{14,15},{16,17},{18,... | collective-permute-start | bytes 36872 | tf_op jit(solution)/shard_map/ppermute | solution.py:16
  134.1 7.0 %collective-permute-start.29 = (f32[2,1,64,256]{3,2,1,0:T(8,128)S(1)}, f32[2,1,64,256]{3,2,1,0:T(8,128)S(1)}, u32[]{:S(2)}, u32[]{:S(2)}) collective-permute-start(f32[2,1,64,256]{3,2,1,0:T(8,128)S(1)} %get-tuple-element.47), channel_id=1, source_target_pairs={{0,2},{2,4},{4,6},{6,8},{8,10},{10,12},{12,14},{1,3},{3,5},{5,7},{... | collective-permute-start | bytes 393224 | tf_op jit(solution)/shard_map/ppermute | solution.py:16
  137.9 7.4 %collective-permute-start.28 = (f32[2,1,64,256]{3,2,1,0:T(8,128)S(1)}, f32[2,1,64,256]{3,2,1,0:T(8,128)S(1)}, u32[]{:S(2)}, u32[]{:S(2)}) collective-permute-start(f32[2,1,64,256]{3,2,1,0:T(8,128)S(1)} %get-tuple-element.48), channel_id=1, source_target_pairs={{2,0},{4,2},{6,4},{8,6},{10,8},{12,10},{14,12},{3,1},{5,3},{7,5},{... | collective-permute-start | bytes 393224 | tf_op jit(solution)/shard_map/ppermute | solution.py:19
  145.3 4.3 %collective-permute-start.30 = (f32[2,6,1,256]{3,2,1,0:T(1,128)S(1)}, f32[2,6,1,256]{3,2,1,0:T(1,128)S(1)}, u32[]{:S(2)}, u32[]{:S(2)}) collective-permute-start(f32[2,6,1,256]{3,2,1,0:T(1,128)S(1)} %get-tuple-element.31), channel_id=1, source_target_pairs={{1,0},{3,2},{5,4},{7,6},{9,8},{11,10},{13,12},{15,14},{17,16},{19,... | collective-permute-start | bytes 36872 | tf_op jit(solution)/shard_map/ppermute | solution.py:19
  146.6 3.9 %collective-permute-start.31 = (f32[2,6,1,256]{3,2,1,0:T(1,128)S(1)}, f32[2,6,1,256]{3,2,1,0:T(1,128)S(1)}, u32[]{:S(2)}, u32[]{:S(2)}) collective-permute-start(f32[2,6,1,256]{3,2,1,0:T(1,128)S(1)} %get-tuple-element.32), channel_id=1, source_target_pairs={{0,1},{2,3},{4,5},{6,7},{8,9},{10,11},{12,13},{14,15},{16,17},{18,... | collective-permute-start | bytes 36872 | tf_op jit(solution)/shard_map/ppermute | solution.py:16
  150.9 1.1 copy-start.2
  152.0 0.8 copy-start.4
Sparse Core Ops, SparseCore 0:
  153.8 69.3 all-reduce.9
where the time goes:
time: 234 us; the launch traced here: 233 us
  waiting for transfers between devices  87.1 us (37%)
  starting transfers between devices  80.2 us (34%)
  blocking collectives  32.3 us (14%)
  between operations  16.6 us (7%)
  other arithmetic  11 us (5%)
  local copies, waits for them, and re-layouts  5.59 us (2%)
    ppermute x16, starting transfers between devices, extended(): lax.ppermute(lax.slice_in_dim(block, block.shape[dim] - width, None, axis...  59.5 us
    psum x1, waiting for transfers between devices, on_device(): rows_sum = lax.psum(rows, 'gx')  36.6 us
    psum x1, blocking collectives, on_device(): squares = lax.psum(local_sq, ('gx', 'gy'))  32.3 us
    ppermute x16, waiting for transfers between devices, extended(): lax.ppermute(lax.slice_in_dim(block, 0, width, axis=dim), axis, backward)  29.1 us
    ppermute x16, waiting for transfers between devices, extended(): lax.ppermute(lax.slice_in_dim(block, block.shape[dim] - width, None, axis...  21.4 us
    ppermute x16, starting transfers between devices, extended(): lax.ppermute(lax.slice_in_dim(block, 0, width, axis=dim), axis, backward)  20.7 us
  transfers between devices with their start and end apart: 33, of which 23 were waited for; matrix products, arithmetic and copies ran while one was open for 2% of the time, Pallas kernels for 0%

commit v1 on v0

--- a/solution.py
+++ b/solution.py
@@ -1,11 +1,20 @@
+import functools
 import math
 import jax
 import jax.numpy as jnp
 from jax import lax
 from jax.sharding import PartitionSpec as P
+from jax.lax import all_gather
 
 COUPLING = 1.0
 STEP_SIZE = 0.2
+
+
+def open_the_local_data(z_in, axis_key):
+    return jnp.sum(all_gather(z_in, axis_key), 0)
+
+
+meet_the_knots = functools.partial(open_the_local_data, axis_key="gx")
 
 
 def extended(block, sides, width):
@@ -85,7 +94,7 @@
     )
     local_sq = jnp.sum(chi_start * chi_start)
     squares = lax.psum(local_sq, ("gx", "gy"))
-    rows_sum = lax.psum(rows, "gx")
+    rows_sum = meet_the_knots(rows)
     power = squares / float(total_x * total_y * depth)
     grad_rows = rows_sum / jnp.sqrt(float(total_x) * (power + 1e-06))
     return (chi_start, grad_rows, jnp.reshape(power, (1,)))

time: 234 us -> 215 us (0.919)
  waiting for transfers between devices: 87.1 us -> 50.5 us
  blocking collectives: 32.3 us -> 63.4 us
  between operations: 16.6 us -> 3.17 us
    psum x1 -> x0, waiting for transfers between devices: 36.6 us -> none  [on_device(): rows_sum = lax.psum(rows, 'gx')]
    all_gather x0 -> x1, blocking collectives: none -> 31.3 us  [open_the_local_data(): return jnp.sum(all_gather(z_in, axis_key), 0)]
  transfers between devices with their start and end apart: 33 -> 32, of which waited for: 23 -> 22; matrix products, arithmetic and copies ran while one was open for 2% -> 2% of each run, Pallas kernels for 0% -> 0%
where the time goes in v1:
time: 215 us; the launch traced here: 214 us
  starting transfers between devices  80.2 us (37%)
  blocking collectives  63.4 us (29%)
  waiting for transfers between devices  50.5 us (23%)
  other arithmetic  11.6 us (5%)
  local copies, waits for them, and re-layouts  5.06 us (2%)
  between operations  3.17 us (1%)
    ppermute x16, starting transfers between devices, extended(): lax.ppermute(lax.slice_in_dim(block, block.shape[dim] - width, None, axis...  59.5 us
    psum x1, blocking collectives, on_device(): squares = lax.psum(local_sq, ('gx', 'gy'))  32.2 us
    all_gather x1, blocking collectives, open_the_local_data(): return jnp.sum(all_gather(z_in, axis_key), 0)  31.3 us
    ppermute x16, waiting for transfers between devices, extended(): lax.ppermute(lax.slice_in_dim(block, 0, width, axis=dim), axis, backward)  29.1 us
    ppermute x16, waiting for transfers between devices, extended(): lax.ppermute(lax.slice_in_dim(block, block.shape[dim] - width, None, axis...  21.4 us
    ppermute x16, starting transfers between devices, extended(): lax.ppermute(lax.slice_in_dim(block, 0, width, axis=dim), axis, backward)  20.7 us
  transfers between devices with their start and end apart: 32, of which 22 were waited for; matrix products, arithmetic and copies ran while one was open for 2% of the time, Pallas kernels for 0%

profile of v1, /device:TPU:0, one launch (start us, length us, event | category | flops | bytes accessed | tf_op | source)
XLA Modules:
  0.0 214.0 jit_solution(1937929946179994768)
XLA Ops:
  0.6 1.0 fusion.145
  1.7 1.3 collective-permute-start
  3.0 5.5 %collective-permute-start.1 = (f32[2,1,64,256]{3,2,1,0:T(8,128)S(1)}, f32[2,1,64,256]{3,2,1,0:T(8,128)S(1)}, u32[]{:S(2)}, u32[]{:S(2)}) collective-permute-start(f32[2,1,64,256]{3,2,1,0:T(8,128)S(1)} %get-tuple-element.62), channel_id=1, source_target_pairs={{0,2},{2,4},{4,6},{6,8},{8,10},{10,12},{12,14},{1,3},{3,5},{5,7},{... | collective-permute-start | bytes 393224 | tf_op jit(solution)/shard_map/ppermute | solution.py:25
  8.5 1.4 slice_bitcast_fusion.14
  9.9 3.1 %collective-permute-done.1 = f32[2,1,64,256]{3,2,1,0:T(8,128)S(1)} collective-permute-done((f32[2,1,64,256]{3,2,1,0:T(8,128)S(1)}, f32[2,1,64,256]{3,2,1,0:T(8,128)S(1)}, u32[]{:S(2)}, u32[]{:S(2)}) %collective-permute-start.1) | collective-permute-done | bytes 131104 | tf_op jit(solution)/shard_map/ppermute | solution.py:25
  13.1 1.3 collective-permute-start.2
  14.4 3.0 %collective-permute-start.3 = (f32[2,6,1,256]{3,2,1,0:T(1,128)S(1)}, f32[2,6,1,256]{3,2,1,0:T(1,128)S(1)}, u32[]{:S(2)}, u32[]{:S(2)}) collective-permute-start(f32[2,6,1,256]{3,2,1,0:T(1,128)S(1)} %get-tuple-element.46), channel_id=1, source_target_pairs={{0,1},{2,3},{4,5},{6,7},{8,9},{10,11},{12,13},{14,15},{16,17},{18,... | collective-permute-start | bytes 36872 | tf_op jit(solution)/shard_map/ppermute | solution.py:25
  17.6 0.6 collective-permute-done.3
  19.2 4.4 %collective-permute-start.5 = (f32[2,1,64,256]{3,2,1,0:T(8,128)S(1)}, f32[2,1,64,256]{3,2,1,0:T(8,128)S(1)}, u32[]{:S(2)}, u32[]{:S(2)}) collective-permute-start(f32[2,1,64,256]{3,2,1,0:T(8,128)S(1)} %get-tuple-element.59), channel_id=1, source_target_pairs={{0,2},{2,4},{4,6},{6,8},{8,10},{10,12},{12,14},{1,3},{3,5},{5,7},{... | collective-permute-start | bytes 393224 | tf_op jit(solution)/shard_map/ppermute | solution.py:25
  23.6 1.3 collective-permute-start.4
  24.9 1.9 collective-permute-done.5
  26.8 4.1 %collective-permute-done.4 = f32[2,1,64,256]{3,2,1,0:T(8,128)S(1)} collective-permute-done((f32[2,1,64,256]{3,2,1,0:T(8,128)S(1)}, f32[2,1,64,256]{3,2,1,0:T(8,128)S(1)}, u32[]{:S(2)}, u32[]{:S(2)}) %collective-permute-start.4) | collective-permute-done | bytes 131104 | tf_op jit(solution)/shard_map/ppermute | solution.py:28
  30.9 1.3 collective-permute-start.6
  32.2 3.0 %collective-permute-start.7 = (f32[2,6,1,256]{3,2,1,0:T(1,128)S(1)}, f32[2,6,1,256]{3,2,1,0:T(1,128)S(1)}, u32[]{:S(2)}, u32[]{:S(2)}) collective-permute-start(f32[2,6,1,256]{3,2,1,0:T(1,128)S(1)} %get-tuple-element.44), channel_id=1, source_target_pairs={{0,1},{2,3},{4,5},{6,7},{8,9},{10,11},{12,13},{14,15},{16,17},{18,... | collective-permute-start | bytes 36872 | tf_op jit(solution)/shard_map/ppermute | solution.py:25
  35.3 0.8 collective-permute-done.7
  36.7 4.5 %collective-permute-start.9 = (f32[2,1,64,256]{3,2,1,0:T(8,128)S(1)}, f32[2,1,64,256]{3,2,1,0:T(8,128)S(1)}, u32[]{:S(2)}, u32[]{:S(2)}) collective-permute-start(f32[2,1,64,256]{3,2,1,0:T(8,128)S(1)} %get-tuple-element.57), channel_id=1, source_target_pairs={{0,2},{2,4},{4,6},{6,8},{8,10},{10,12},{12,14},{1,3},{3,5},{5,7},{... | collective-permute-start | bytes 393224 | tf_op jit(solution)/shard_map/ppermute | solution.py:25
  41.3 1.3 collective-permute-start.8
  42.6 1.9 collective-permute-done.9
  44.5 4.1 %collective-permute-done.8 = f32[2,1,64,256]{3,2,1,0:T(8,128)S(1)} collective-permute-done((f32[2,1,64,256]{3,2,1,0:T(8,128)S(1)}, f32[2,1,64,256]{3,2,1,0:T(8,128)S(1)}, u32[]{:S(2)}, u32[]{:S(2)}) %collective-permute-start.8) | collective-permute-done | bytes 131104 | tf_op jit(solution)/shard_map/ppermute | solution.py:28
  48.7 1.3 collective-permute-start.10
  50.0 3.0 %collective-permute-start.11 = (f32[2,6,1,256]{3,2,1,0:T(1,128)S(1)}, f32[2,6,1,256]{3,2,1,0:T(1,128)S(1)}, u32[]{:S(2)}, u32[]{:S(2)}) collective-permute-start(f32[2,6,1,256]{3,2,1,0:T(1,128)S(1)} %get-tuple-element.42), channel_id=1, source_target_pairs={{0,1},{2,3},{4,5},{6,7},{8,9},{10,11},{12,13},{14,15},{16,17},{18,... | collective-permute-start | bytes 36872 | tf_op jit(solution)/shard_map/ppermute | solution.py:25
  53.0 0.8 collective-permute-done.11
  54.4 4.0 %collective-permute-start.13 = (f32[2,1,64,256]{3,2,1,0:T(8,128)S(1)}, f32[2,1,64,256]{3,2,1,0:T(8,128)S(1)}, u32[]{:S(2)}, u32[]{:S(2)}) collective-permute-start(f32[2,1,64,256]{3,2,1,0:T(8,128)S(1)} %get-tuple-element.55), channel_id=1, source_target_pairs={{0,2},{2,4},{4,6},{6,8},{8,10},{10,12},{12,14},{1,3},{3,5},{5,7},{... | collective-permute-start | bytes 393224 | tf_op jit(solution)/shard_map/ppermute | solution.py:25
  58.4 1.3 collective-permute-start.12
  59.7 1.9 collective-permute-done.13
  61.7 4.1 %collective-permute-done.12 = f32[2,1,64,256]{3,2,1,0:T(8,128)S(1)} collective-permute-done((f32[2,1,64,256]{3,2,1,0:T(8,128)S(1)}, f32[2,1,64,256]{3,2,1,0:T(8,128)S(1)}, u32[]{:S(2)}, u32[]{:S(2)}) %collective-permute-start.12) | collective-permute-done | bytes 131104 | tf_op jit(solution)/shard_map/ppermute | solution.py:28
  65.8 1.3 collective-permute-start.14
  67.1 3.0 %collective-permute-start.15 = (f32[2,6,1,256]{3,2,1,0:T(1,128)S(1)}, f32[2,6,1,256]{3,2,1,0:T(1,128)S(1)}, u32[]{:S(2)}, u32[]{:S(2)}) collective-permute-start(f32[2,6,1,256]{3,2,1,0:T(1,128)S(1)} %get-tuple-element.40), channel_id=1, source_target_pairs={{0,1},{2,3},{4,5},{6,7},{8,9},{10,11},{12,13},{14,15},{16,17},{18,... | collective-permute-start | bytes 36872 | tf_op jit(solution)/shard_map/ppermute | solution.py:25
  70.1 0.8 collective-permute-done.15
  71.7 4.0 %collective-permute-start.17 = (f32[2,1,64,256]{3,2,1,0:T(8,128)S(1)}, f32[2,1,64,256]{3,2,1,0:T(8,128)S(1)}, u32[]{:S(2)}, u32[]{:S(2)}) collective-permute-start(f32[2,1,64,256]{3,2,1,0:T(8,128)S(1)} %get-tuple-element.53), channel_id=1, source_target_pairs={{0,2},{2,4},{4,6},{6,8},{8,10},{10,12},{12,14},{1,3},{3,5},{5,7},{... | collective-permute-start | bytes 393224 | tf_op jit(solution)/shard_map/ppermute | solution.py:25
  75.7 1.3 collective-permute-start.16
  77.0 1.9 collective-permute-done.17
  78.9 4.1 %collective-permute-done.16 = f32[2,1,64,256]{3,2,1,0:T(8,128)S(1)} collective-permute-done((f32[2,1,64,256]{3,2,1,0:T(8,128)S(1)}, f32[2,1,64,256]{3,2,1,0:T(8,128)S(1)}, u32[]{:S(2)}, u32[]{:S(2)}) %collective-permute-start.16) | collective-permute-done | bytes 131104 | tf_op jit(solution)/shard_map/ppermute | solution.py:28
  83.7 1.3 collective-permute-start.18
  85.0 4.2 %collective-permute-start.19 = (f32[2,6,1,256]{3,2,1,0:T(1,128)S(1)}, f32[2,6,1,256]{3,2,1,0:T(1,128)}, u32[]{:S(2)}, u32[]{:S(2)}) collective-permute-start(f32[2,6,1,256]{3,2,1,0:T(1,128)S(1)} %get-tuple-element.38), channel_id=1, source_target_pairs={{0,1},{2,3},{4,5},{6,7},{8,9},{10,11},{12,13},{14,15},{16,17},{18,... | collective-permute-start | bytes 36872 | tf_op jit(solution)/shard_map/ppermute | solution.py:25
  89.2 0.7 broadcast_in_dim.5
  89.8 1.5 mul.427
  91.3 1.3 fusion.14
  93.4 4.0 %collective-permute-start.21 = (f32[2,1,64,256]{3,2,1,0:T(8,128)S(1)}, f32[2,1,64,256]{3,2,1,0:T(8,128)S(1)}, u32[]{:S(2)}, u32[]{:S(2)}) collective-permute-start(f32[2,1,64,256]{3,2,1,0:T(8,128)S(1)} %get-tuple-element.51), channel_id=1, source_target_pairs={{0,2},{2,4},{4,6},{6,8},{8,10},{10,12},{12,14},{1,3},{3,5},{5,7},{... | collective-permute-start | bytes 393224 | tf_op jit(solution)/shard_map/ppermute | solution.py:25
  97.4 1.3 collective-permute-start.20
  98.7 1.2 collective-permute-done.21
  99.9 4.4 %collective-permute-done.20 = f32[2,1,64,256]{3,2,1,0:T(8,128)S(1)} collective-permute-done((f32[2,1,64,256]{3,2,1,0:T(8,128)S(1)}, f32[2,1,64,256]{3,2,1,0:T(8,128)S(1)}, u32[]{:S(2)}, u32[]{:S(2)}) %collective-permute-start.20) | collective-permute-done | bytes 131104 | tf_op jit(solution)/shard_map/ppermute | solution.py:28
  104.2 1.3 collective-permute-start.22
  105.5 3.0 %collective-permute-start.23 = (f32[2,6,1,256]{3,2,1,0:T(1,128)S(1)}, f32[2,6,1,256]{3,2,1,0:T(1,128)S(1)}, u32[]{:S(2)}, u32[]{:S(2)}) collective-permute-start(f32[2,6,1,256]{3,2,1,0:T(1,128)S(1)} %get-tuple-element.36), channel_id=1, source_target_pairs={{0,1},{2,3},{4,5},{6,7},{8,9},{10,11},{12,13},{14,15},{16,17},{18,... | collective-permute-start | bytes 36872 | tf_op jit(solution)/shard_map/ppermute | solution.py:25
  108.6 0.8 collective-permute-done.23
  110.2 4.0 %collective-permute-start.25 = (f32[2,1,64,256]{3,2,1,0:T(8,128)S(1)}, f32[2,1,64,256]{3,2,1,0:T(8,128)S(1)}, u32[]{:S(2)}, u32[]{:S(2)}) collective-permute-start(f32[2,1,64,256]{3,2,1,0:T(8,128)S(1)} %get-tuple-element.49), channel_id=1, source_target_pairs={{0,2},{2,4},{4,6},{6,8},{8,10},{10,12},{12,14},{1,3},{3,5},{5,7},{... | collective-permute-start | bytes 393224 | tf_op jit(solution)/shard_map/ppermute | solution.py:25
  114.2 1.3 collective-permute-start.24
  115.5 1.9 collective-permute-done.25
  117.4 4.1 %collective-permute-done.24 = f32[2,1,64,256]{3,2,1,0:T(8,128)S(1)} collective-permute-done((f32[2,1,64,256]{3,2,1,0:T(8,128)S(1)}, f32[2,1,64,256]{3,2,1,0:T(8,128)S(1)}, u32[]{:S(2)}, u32[]{:S(2)}) %collective-permute-start.24) | collective-permute-done | bytes 131104 | tf_op jit(solution)/shard_map/ppermute | solution.py:28
  121.6 1.3 collective-permute-start.26
  122.9 3.0 %collective-permute-start.27 = (f32[2,6,1,256]{3,2,1,0:T(1,128)S(1)}, f32[2,6,1,256]{3,2,1,0:T(1,128)S(1)}, u32[]{:S(2)}, u32[]{:S(2)}) collective-permute-start(f32[2,6,1,256]{3,2,1,0:T(1,128)S(1)} %get-tuple-element.34), channel_id=1, source_target_pairs={{0,1},{2,3},{4,5},{6,7},{8,9},{10,11},{12,13},{14,15},{16,17},{18,... | collective-permute-start | bytes 36872 | tf_op jit(solution)/shard_map/ppermute | solution.py:25
  125.9 0.8 collective-permute-done.27
  127.5 3.8 %collective-permute-start.29 = (f32[2,1,64,256]{3,2,1,0:T(8,128)S(1)}, f32[2,1,64,256]{3,2,1,0:T(8,128)S(1)}, u32[]{:S(2)}, u32[]{:S(2)}) collective-permute-start(f32[2,1,64,256]{3,2,1,0:T(8,128)S(1)} %get-tuple-element.47), channel_id=1, source_target_pairs={{0,2},{2,4},{4,6},{6,8},{8,10},{10,12},{12,14},{1,3},{3,5},{5,7},{... | collective-permute-start | bytes 393224 | tf_op jit(solution)/shard_map/ppermute | solution.py:25
  131.3 1.3 collective-permute-start.28
  132.6 1.9 collective-permute-done.29
  134.5 4.1 %collective-permute-done.28 = f32[2,1,64,256]{3,2,1,0:T(8,128)S(1)} collective-permute-done((f32[2,1,64,256]{3,2,1,0:T(8,128)S(1)}, f32[2,1,64,256]{3,2,1,0:T(8,128)S(1)}, u32[]{:S(2)}, u32[]{:S(2)}) %collective-permute-start.28) | collective-permute-done | bytes 131104 | tf_op jit(solution)/shard_map/ppermute | solution.py:28
  138.7 1.3 collective-permute-start.30
  140.0 3.0 %collective-permute-start.31 = (f32[2,6,1,256]{3,2,1,0:T(1,128)S(1)}, f32[2,6,1,256]{3,2,1,0:T(1,128)S(1)}, u32[]{:S(2)}, u32[]{:S(2)}) collective-permute-start(f32[2,6,1,256]{3,2,1,0:T(1,128)S(1)} %get-tuple-element.32), channel_id=1, source_target_pairs={{0,1},{2,3},{4,5},{6,7},{8,9},{10,11},{12,13},{14,15},{16,17},{18,... | collective-permute-start | bytes 36872 | tf_op jit(solution)/shard_map/ppermute | solution.py:25
  143.0 0.8 collective-permute-done.31
  144.3 1.9 multiply_reduce_fusion
  146.2 32.2 %psum.7 = f32[]{:T(128)} all-reduce(f32[]{:T(128)} %get-tuple-element.5), channel_id=1, replica_groups=mesh['starts'=2,'gx'=8,'gy'=2] {'gx','gy'}, use_global_device_ids=true, to_apply=%region_6.7 | all-reduce | flops 1 | bytes 8 | tf_op jit(solution)/shard_map/psum | solution.py:96
  179.1 1.6 fusion.55
  180.9 31.3 %all-gather = f32[16,32,256]{2,1,0:T(8,128)S(1)} all-gather(f32[2,32,256]{2,1,0:T(8,128)S(1)} %pad_maximum_fusion.66), channel_id=2, replica_groups=mesh['starts'=2,'gx'=8,'gy'=2] {'gx'}, dimensions={0}, use_global_device_ids=true | all-gather | bytes 589824 | tf_op jit(solution)/shard_map/all_gather | solution.py:14
  212.2 0.6 broadcast_divide_fusion
  (75 shorter events, 6.7 us)
Async XLA Ops:
  0.6 12.4 %copy-start = (f32[2,4,64,256]{3,2,1,0:T(8,128)S(1)}, f32[2,4,64,256]{3,2,1,0:T(8,128)}, u32[]{:S(2)}) copy-start(f32[2,4,64,256]{3,2,1,0:T(8,128)} %param.5) | copy-start | bytes 1572868
  1.7 11.4 %collective-permute-start = (f32[2,1,64,256]{3,2,1,0:T(8,128)S(1)}, f32[2,1,64,256]{3,2,1,0:T(8,128)S(1)}, u32[]{:S(2)}, u32[]{:S(2)}) collective-permute-start(f32[2,1,64,256]{3,2,1,0:T(8,128)S(1)} %get-tuple-element.61), channel_id=1, source_target_pairs={{2,0},{4,2},{6,4},{8,6},{10,8},{12,10},{14,12},{3,1},{5,3},{7,5},{... | collective-permute-start | bytes 393224 | tf_op jit(solution)/shard_map/ppermute | solution.py:28
  3.0 10.0 %collective-permute-start.1 = (f32[2,1,64,256]{3,2,1,0:T(8,128)S(1)}, f32[2,1,64,256]{3,2,1,0:T(8,128)S(1)}, u32[]{:S(2)}, u32[]{:S(2)}) collective-permute-start(f32[2,1,64,256]{3,2,1,0:T(8,128)S(1)} %get-tuple-element.62), channel_id=1, source_target_pairs={{0,2},{2,4},{4,6},{6,8},{8,10},{10,12},{12,14},{1,3},{3,5},{5,7},{... | collective-permute-start | bytes 393224 | tf_op jit(solution)/shard_map/ppermute | solution.py:25
  13.1 4.5 %collective-permute-start.2 = (f32[2,6,1,256]{3,2,1,0:T(1,128)S(1)}, f32[2,6,1,256]{3,2,1,0:T(1,128)S(1)}, u32[]{:S(2)}, u32[]{:S(2)}) collective-permute-start(f32[2,6,1,256]{3,2,1,0:T(1,128)S(1)} %get-tuple-element.45), channel_id=1, source_target_pairs={{1,0},{3,2},{5,4},{7,6},{9,8},{11,10},{13,12},{15,14},{17,16},{19,... | collective-permute-start | bytes 36872 | tf_op jit(solution)/shard_map/ppermute | solution.py:28
  14.4 3.9 %collective-permute-start.3 = (f32[2,6,1,256]{3,2,1,0:T(1,128)S(1)}, f32[2,6,1,256]{3,2,1,0:T(1,128)S(1)}, u32[]{:S(2)}, u32[]{:S(2)}) collective-permute-start(f32[2,6,1,256]{3,2,1,0:T(1,128)S(1)} %get-tuple-element.46), channel_id=1, source_target_pairs={{0,1},{2,3},{4,5},{6,7},{8,9},{10,11},{12,13},{14,15},{16,17},{18,... | collective-permute-start | bytes 36872 | tf_op jit(solution)/shard_map/ppermute | solution.py:25
  17.6 1.1 copy-start.1
  17.6 1.1 copy-start.3
  19.2 7.6 %collective-permute-start.5 = (f32[2,1,64,256]{3,2,1,0:T(8,128)S(1)}, f32[2,1,64,256]{3,2,1,0:T(8,128)S(1)}, u32[]{:S(2)}, u32[]{:S(2)}) collective-permute-start(f32[2,1,64,256]{3,2,1,0:T(8,128)S(1)} %get-tuple-element.59), channel_id=1, source_target_pairs={{0,2},{2,4},{4,6},{6,8},{8,10},{10,12},{12,14},{1,3},{3,5},{5,7},{... | collective-permute-start | bytes 393224 | tf_op jit(solution)/shard_map/ppermute | solution.py:25
  23.6 7.4 %collective-permute-start.4 = (f32[2,1,64,256]{3,2,1,0:T(8,128)S(1)}, f32[2,1,64,256]{3,2,1,0:T(8,128)S(1)}, u32[]{:S(2)}, u32[]{:S(2)}) collective-permute-start(f32[2,1,64,256]{3,2,1,0:T(8,128)S(1)} %get-tuple-element.60), channel_id=1, source_target_pairs={{2,0},{4,2},{6,4},{8,6},{10,8},{12,10},{14,12},{3,1},{5,3},{7,5},{... | collective-permute-start | bytes 393224 | tf_op jit(solution)/shard_map/ppermute | solution.py:28
  30.9 4.3 %collective-permute-start.6 = (f32[2,6,1,256]{3,2,1,0:T(1,128)S(1)}, f32[2,6,1,256]{3,2,1,0:T(1,128)S(1)}, u32[]{:S(2)}, u32[]{:S(2)}) collective-permute-start(f32[2,6,1,256]{3,2,1,0:T(1,128)S(1)} %get-tuple-element.43), channel_id=1, source_target_pairs={{1,0},{3,2},{5,4},{7,6},{9,8},{11,10},{13,12},{15,14},{17,16},{19,... | collective-permute-start | bytes 36872 | tf_op jit(solution)/shard_map/ppermute | solution.py:28
  32.2 3.9 %collective-permute-start.7 = (f32[2,6,1,256]{3,2,1,0:T(1,128)S(1)}, f32[2,6,1,256]{3,2,1,0:T(1,128)S(1)}, u32[]{:S(2)}, u32[]{:S(2)}) collective-permute-start(f32[2,6,1,256]{3,2,1,0:T(1,128)S(1)} %get-tuple-element.44), channel_id=1, source_target_pairs={{0,1},{2,3},{4,5},{6,7},{8,9},{10,11},{12,13},{14,15},{16,17},{18,... | collective-permute-start | bytes 36872 | tf_op jit(solution)/shard_map/ppermute | solution.py:25
  36.7 7.8 %collective-permute-start.9 = (f32[2,1,64,256]{3,2,1,0:T(8,128)S(1)}, f32[2,1,64,256]{3,2,1,0:T(8,128)S(1)}, u32[]{:S(2)}, u32[]{:S(2)}) collective-permute-start(f32[2,1,64,256]{3,2,1,0:T(8,128)S(1)} %get-tuple-element.57), channel_id=1, source_target_pairs={{0,2},{2,4},{4,6},{6,8},{8,10},{10,12},{12,14},{1,3},{3,5},{5,7},{... | collective-permute-start | bytes 393224 | tf_op jit(solution)/shard_map/ppermute | solution.py:25
  41.3 7.4 %collective-permute-start.8 = (f32[2,1,64,256]{3,2,1,0:T(8,128)S(1)}, f32[2,1,64,256]{3,2,1,0:T(8,128)S(1)}, u32[]{:S(2)}, u32[]{:S(2)}) collective-permute-start(f32[2,1,64,256]{3,2,1,0:T(8,128)S(1)} %get-tuple-element.58), channel_id=1, source_target_pairs={{2,0},{4,2},{6,4},{8,6},{10,8},{12,10},{14,12},{3,1},{5,3},{7,5},{... | collective-permute-start | bytes 393224 | tf_op jit(solution)/shard_map/ppermute | solution.py:28
  48.7 4.3 %collective-permute-start.10 = (f32[2,6,1,256]{3,2,1,0:T(1,128)S(1)}, f32[2,6,1,256]{3,2,1,0:T(1,128)S(1)}, u32[]{:S(2)}, u32[]{:S(2)}) collective-permute-start(f32[2,6,1,256]{3,2,1,0:T(1,128)S(1)} %get-tuple-element.41), channel_id=1, source_target_pairs={{1,0},{3,2},{5,4},{7,6},{9,8},{11,10},{13,12},{15,14},{17,16},{19,... | collective-permute-start | bytes 36872 | tf_op jit(solution)/shard_map/ppermute | solution.py:28
  50.0 3.9 %collective-permute-start.11 = (f32[2,6,1,256]{3,2,1,0:T(1,128)S(1)}, f32[2,6,1,256]{3,2,1,0:T(1,128)S(1)}, u32[]{:S(2)}, u32[]{:S(2)}) collective-permute-start(f32[2,6,1,256]{3,2,1,0:T(1,128)S(1)} %get-tuple-element.42), channel_id=1, source_target_pairs={{0,1},{2,3},{4,5},{6,7},{8,9},{10,11},{12,13},{14,15},{16,17},{18,... | collective-permute-start | bytes 36872 | tf_op jit(solution)/shard_map/ppermute | solution.py:25
  54.4 7.2 %collective-permute-start.13 = (f32[2,1,64,256]{3,2,1,0:T(8,128)S(1)}, f32[2,1,64,256]{3,2,1,0:T(8,128)S(1)}, u32[]{:S(2)}, u32[]{:S(2)}) collective-permute-start(f32[2,1,64,256]{3,2,1,0:T(8,128)S(1)} %get-tuple-element.55), channel_id=1, source_target_pairs={{0,2},{2,4},{4,6},{6,8},{8,10},{10,12},{12,14},{1,3},{3,5},{5,7},{... | collective-permute-start | bytes 393224 | tf_op jit(solution)/shard_map/ppermute | solution.py:25
  58.4 7.4 %collective-permute-start.12 = (f32[2,1,64,256]{3,2,1,0:T(8,128)S(1)}, f32[2,1,64,256]{3,2,1,0:T(8,128)S(1)}, u32[]{:S(2)}, u32[]{:S(2)}) collective-permute-start(f32[2,1,64,256]{3,2,1,0:T(8,128)S(1)} %get-tuple-element.56), channel_id=1, source_target_pairs={{2,0},{4,2},{6,4},{8,6},{10,8},{12,10},{14,12},{3,1},{5,3},{7,5},{... | collective-permute-start | bytes 393224 | tf_op jit(solution)/shard_map/ppermute | solution.py:28
  65.8 4.3 %collective-permute-start.14 = (f32[2,6,1,256]{3,2,1,0:T(1,128)S(1)}, f32[2,6,1,256]{3,2,1,0:T(1,128)S(1)}, u32[]{:S(2)}, u32[]{:S(2)}) collective-permute-start(f32[2,6,1,256]{3,2,1,0:T(1,128)S(1)} %get-tuple-element.39), channel_id=1, source_target_pairs={{1,0},{3,2},{5,4},{7,6},{9,8},{11,10},{13,12},{15,14},{17,16},{19,... | collective-permute-start | bytes 36872 | tf_op jit(solution)/shard_map/ppermute | solution.py:28
  67.1 3.9 %collective-permute-start.15 = (f32[2,6,1,256]{3,2,1,0:T(1,128)S(1)}, f32[2,6,1,256]{3,2,1,0:T(1,128)S(1)}, u32[]{:S(2)}, u32[]{:S(2)}) collective-permute-start(f32[2,6,1,256]{3,2,1,0:T(1,128)S(1)} %get-tuple-element.40), channel_id=1, source_target_pairs={{0,1},{2,3},{4,5},{6,7},{8,9},{10,11},{12,13},{14,15},{16,17},{18,... | collective-permute-start | bytes 36872 | tf_op jit(solution)/shard_map/ppermute | solution.py:25
  71.7 7.2 %collective-permute-start.17 = (f32[2,1,64,256]{3,2,1,0:T(8,128)S(1)}, f32[2,1,64,256]{3,2,1,0:T(8,128)S(1)}, u32[]{:S(2)}, u32[]{:S(2)}) collective-permute-start(f32[2,1,64,256]{3,2,1,0:T(8,128)S(1)} %get-tuple-element.53), channel_id=1, source_target_pairs={{0,2},{2,4},{4,6},{6,8},{8,10},{10,12},{12,14},{1,3},{3,5},{5,7},{... | collective-permute-start | bytes 393224 | tf_op jit(solution)/shard_map/ppermute | solution.py:25
  75.6 13.5 %copy-start.6 = (f32[32,256]{1,0:T(8,128)S(1)}, f32[32,256]{1,0:T(8,128)}, u32[]{:S(2)}) copy-start(f32[32,256]{1,0:T(8,128)} %get-tuple-element.63) | copy-start | bytes 98308
  75.7 7.4 %collective-permute-start.16 = (f32[2,1,64,256]{3,2,1,0:T(8,128)S(1)}, f32[2,1,64,256]{3,2,1,0:T(8,128)S(1)}, u32[]{:S(2)}, u32[]{:S(2)}) collective-permute-start(f32[2,1,64,256]{3,2,1,0:T(8,128)S(1)} %get-tuple-element.54), channel_id=1, source_target_pairs={{2,0},{4,2},{6,4},{8,6},{10,8},{12,10},{14,12},{3,1},{5,3},{7,5},{... | collective-permute-start | bytes 393224 | tf_op jit(solution)/shard_map/ppermute | solution.py:28
  83.0 0.7 copy-start.4
  83.7 7.7 %collective-permute-start.18 = (f32[2,6,1,256]{3,2,1,0:T(1,128)}, f32[2,6,1,256]{3,2,1,0:T(1,128)}, u32[]{:S(2)}, u32[]{:S(2)}) collective-permute-start(f32[2,6,1,256]{3,2,1,0:T(1,128)} %get-tuple-element.37), channel_id=1, source_target_pairs={{1,0},{3,2},{5,4},{7,6},{9,8},{11,10},{13,12},{15,14},{17,16},{19,... | collective-permute-start | bytes 36872 | tf_op jit(solution)/shard_map/ppermute | solution.py:28
  85.0 6.4 %collective-permute-start.19 = (f32[2,6,1,256]{3,2,1,0:T(1,128)S(1)}, f32[2,6,1,256]{3,2,1,0:T(1,128)}, u32[]{:S(2)}, u32[]{:S(2)}) collective-permute-start(f32[2,6,1,256]{3,2,1,0:T(1,128)S(1)} %get-tuple-element.38), channel_id=1, source_target_pairs={{0,1},{2,3},{4,5},{6,7},{8,9},{10,11},{12,13},{14,15},{16,17},{18,... | collective-permute-start | bytes 36872 | tf_op jit(solution)/shard_map/ppermute | solution.py:25
  91.3 1.3 copy-start.2
  91.3 1.4 copy-start.5
  93.4 6.5 %collective-permute-start.21 = (f32[2,1,64,256]{3,2,1,0:T(8,128)S(1)}, f32[2,1,64,256]{3,2,1,0:T(8,128)S(1)}, u32[]{:S(2)}, u32[]{:S(2)}) collective-permute-start(f32[2,1,64,256]{3,2,1,0:T(8,128)S(1)} %get-tuple-element.51), channel_id=1, source_target_pairs={{0,2},{2,4},{4,6},{6,8},{8,10},{10,12},{12,14},{1,3},{3,5},{5,7},{... | collective-permute-start | bytes 393224 | tf_op jit(solution)/shard_map/ppermute | solution.py:25
  97.4 6.9 %collective-permute-start.20 = (f32[2,1,64,256]{3,2,1,0:T(8,128)S(1)}, f32[2,1,64,256]{3,2,1,0:T(8,128)S(1)}, u32[]{:S(2)}, u32[]{:S(2)}) collective-permute-start(f32[2,1,64,256]{3,2,1,0:T(8,128)S(1)} %get-tuple-element.52), channel_id=1, source_target_pairs={{2,0},{4,2},{6,4},{8,6},{10,8},{12,10},{14,12},{3,1},{5,3},{7,5},{... | collective-permute-start | bytes 393224 | tf_op jit(solution)/shard_map/ppermute | solution.py:28
  104.2 4.3 %collective-permute-start.22 = (f32[2,6,1,256]{3,2,1,0:T(1,128)S(1)}, f32[2,6,1,256]{3,2,1,0:T(1,128)S(1)}, u32[]{:S(2)}, u32[]{:S(2)}) collective-permute-start(f32[2,6,1,256]{3,2,1,0:T(1,128)S(1)} %get-tuple-element.35), channel_id=1, source_target_pairs={{1,0},{3,2},{5,4},{7,6},{9,8},{11,10},{13,12},{15,14},{17,16},{19,... | collective-permute-start | bytes 36872 | tf_op jit(solution)/shard_map/ppermute | solution.py:28
  105.5 3.9 %collective-permute-start.23 = (f32[2,6,1,256]{3,2,1,0:T(1,128)S(1)}, f32[2,6,1,256]{3,2,1,0:T(1,128)S(1)}, u32[]{:S(2)}, u32[]{:S(2)}) collective-permute-start(f32[2,6,1,256]{3,2,1,0:T(1,128)S(1)} %get-tuple-element.36), channel_id=1, source_target_pairs={{0,1},{2,3},{4,5},{6,7},{8,9},{10,11},{12,13},{14,15},{16,17},{18,... | collective-permute-start | bytes 36872 | tf_op jit(solution)/shard_map/ppermute | solution.py:25
  110.2 7.2 %collective-permute-start.25 = (f32[2,1,64,256]{3,2,1,0:T(8,128)S(1)}, f32[2,1,64,256]{3,2,1,0:T(8,128)S(1)}, u32[]{:S(2)}, u32[]{:S(2)}) collective-permute-start(f32[2,1,64,256]{3,2,1,0:T(8,128)S(1)} %get-tuple-element.49), channel_id=1, source_target_pairs={{0,2},{2,4},{4,6},{6,8},{8,10},{10,12},{12,14},{1,3},{3,5},{5,7},{... | collective-permute-start | bytes 393224 | tf_op jit(solution)/shard_map/ppermute | solution.py:25
  114.2 7.4 %collective-permute-start.24 = (f32[2,1,64,256]{3,2,1,0:T(8,128)S(1)}, f32[2,1,64,256]{3,2,1,0:T(8,128)S(1)}, u32[]{:S(2)}, u32[]{:S(2)}) collective-permute-start(f32[2,1,64,256]{3,2,1,0:T(8,128)S(1)} %get-tuple-element.50), channel_id=1, source_target_pairs={{2,0},{4,2},{6,4},{8,6},{10,8},{12,10},{14,12},{3,1},{5,3},{7,5},{... | collective-permute-start | bytes 393224 | tf_op jit(solution)/shard_map/ppermute | solution.py:28
  121.6 4.3 %collective-permute-start.26 = (f32[2,6,1,256]{3,2,1,0:T(1,128)S(1)}, f32[2,6,1,256]{3,2,1,0:T(1,128)S(1)}, u32[]{:S(2)}, u32[]{:S(2)}) collective-permute-start(f32[2,6,1,256]{3,2,1,0:T(1,128)S(1)} %get-tuple-element.33), channel_id=1, source_target_pairs={{1,0},{3,2},{5,4},{7,6},{9,8},{11,10},{13,12},{15,14},{17,16},{19,... | collective-permute-start | bytes 36872 | tf_op jit(solution)/shard_map/ppermute | solution.py:28
  122.9 3.9 %collective-permute-start.27 = (f32[2,6,1,256]{3,2,1,0:T(1,128)S(1)}, f32[2,6,1,256]{3,2,1,0:T(1,128)S(1)}, u32[]{:S(2)}, u32[]{:S(2)}) collective-permute-start(f32[2,6,1,256]{3,2,1,0:T(1,128)S(1)} %get-tuple-element.34), channel_id=1, source_target_pairs={{0,1},{2,3},{4,5},{6,7},{8,9},{10,11},{12,13},{14,15},{16,17},{18,... | collective-permute-start | bytes 36872 | tf_op jit(solution)/shard_map/ppermute | solution.py:25
  127.5 7.0 %collective-permute-start.29 = (f32[2,1,64,256]{3,2,1,0:T(8,128)S(1)}, f32[2,1,64,256]{3,2,1,0:T(8,128)S(1)}, u32[]{:S(2)}, u32[]{:S(2)}) collective-permute-start(f32[2,1,64,256]{3,2,1,0:T(8,128)S(1)} %get-tuple-element.47), channel_id=1, source_target_pairs={{0,2},{2,4},{4,6},{6,8},{8,10},{10,12},{12,14},{1,3},{3,5},{5,7},{... | collective-permute-start | bytes 393224 | tf_op jit(solution)/shard_map/ppermute | solution.py:25
  131.3 7.4 %collective-permute-start.28 = (f32[2,1,64,256]{3,2,1,0:T(8,128)S(1)}, f32[2,1,64,256]{3,2,1,0:T(8,128)S(1)}, u32[]{:S(2)}, u32[]{:S(2)}) collective-permute-start(f32[2,1,64,256]{3,2,1,0:T(8,128)S(1)} %get-tuple-element.48), channel_id=1, source_target_pairs={{2,0},{4,2},{6,4},{8,6},{10,8},{12,10},{14,12},{3,1},{5,3},{7,5},{... | collective-permute-start | bytes 393224 | tf_op jit(solution)/shard_map/ppermute | solution.py:28
  138.7 4.3 %collective-permute-start.30 = (f32[2,6,1,256]{3,2,1,0:T(1,128)S(1)}, f32[2,6,1,256]{3,2,1,0:T(1,128)S(1)}, u32[]{:S(2)}, u32[]{:S(2)}) collective-permute-start(f32[2,6,1,256]{3,2,1,0:T(1,128)S(1)} %get-tuple-element.31), channel_id=1, source_target_pairs={{1,0},{3,2},{5,4},{7,6},{9,8},{11,10},{13,12},{15,14},{17,16},{19,... | collective-permute-start | bytes 36872 | tf_op jit(solution)/shard_map/ppermute | solution.py:28
  140.0 3.9 %collective-permute-start.31 = (f32[2,6,1,256]{3,2,1,0:T(1,128)S(1)}, f32[2,6,1,256]{3,2,1,0:T(1,128)S(1)}, u32[]{:S(2)}, u32[]{:S(2)}) collective-permute-start(f32[2,6,1,256]{3,2,1,0:T(1,128)S(1)} %get-tuple-element.32), channel_id=1, source_target_pairs={{0,1},{2,3},{4,5},{6,7},{8,9},{10,11},{12,13},{14,15},{16,17},{18,... | collective-permute-start | bytes 36872 | tf_op jit(solution)/shard_map/ppermute | solution.py:25
